TPU v7x, 512 devices: a whole 4x4x16 slice. The times are simulated.
512 devices in a mesh: ctx: 64 (over z, x_hi, core), head: 8 (over y, x_lo).
Axes of the slice: x: 4 (x_hi: 2, x_lo: 2; x = x_hi * 2 + x_lo), y: 4, z: 16, core: 2. Of those that a mesh axis runs over, the one named last changes fastest.
Arguments:
- tokens: bfloat16 [8192, 4096], P('ctx'), may hold values from -6 to 6
- norm_gain: float32 [4096], replicated, may hold values from 0.25 to 1.75
- w_query: bfloat16 [4096, 4096], P('ctx', 'head'), may hold values from -0.09375 to 0.09375
- w_key: bfloat16 [4096, 1024], P('ctx', 'head'), may hold values from -0.09375 to 0.09375
- w_value: bfloat16 [4096, 1024], P('ctx', 'head'), may hold values from -0.09375 to 0.09375
- w_out: bfloat16 [4096, 4096], P('head', 'ctx'), may hold values from -0.09375 to 0.09375
- row_map: int32 [8192], P('ctx'), may hold values from 0 to 8191, as said below
- doc_lengths: int32 [32], replicated, may hold values from 1 to 2048, 8192 in all
- doc_labels: int32 [32], replicated, may hold values from 0 to 1, as said below
Outputs:
- residual_out: bfloat16 [8192, 4096], P('ctx', 'head')
- refusal_direction: float32 [4096], P('head')
Inputs may be any that keep to these rules, and one draw needn't show every extreme that they name: `row_map`: the rows of ctx index c are two runs of 64 consecutive positions, run b(c) and run 2 * 64 - 1 - b(c) of the pack, b a permutation drawn from the seed; every position appears once. `doc_labels`: at least one prompt of each class.
All inputs are finite; a program needn't handle non-finite values.
Results may differ from a plain program's by a relative error of at most 0.008.
Values may be sent and summed in bfloat16 or wider, within the bound.
No kernel may reach another device: no remote copies, remote signals or barrier semaphores. Data moves between devices by JAX's collectives and lax.ppermute only.
A program may use at most 64 MiB of HBM per device.

v0:
```python
import math
import jax
import jax.numpy as jnp
from jax import lax
from jax.sharding import PartitionSpec as P

HEADS = 32
KV_HEADS = 8
HEAD_DIM = 128
ROPE_BASE = 500000.0
NEG_FILL = -1e30
BLOCK_KEYS = 512


def doc_layout(row_map, doc_lengths):
    doc_ends = jnp.cumsum(doc_lengths)
    doc_starts = doc_ends - doc_lengths
    doc_index = jnp.sum((row_map[:, None] >= doc_ends[None, :]).astype(jnp.int32), 1)
    member = doc_index[:, None] == jnp.arange(doc_ends.shape[0], dtype=jnp.int32)[None, :]
    in_doc = row_map - jnp.sum(jnp.where(member, doc_starts[None, :], 0), 1)
    return (doc_index, in_doc, doc_ends)


def rotate(values, in_doc):
    head_dim = values.shape[-1]
    half_dim = head_dim // 2
    inv_freq = jnp.exp(
        jnp.arange(half_dim).astype(jnp.float32) * (-2.0 * math.log(ROPE_BASE) / head_dim)
    )
    angles = in_doc.astype(jnp.float32)[:, None] * inv_freq[None, :]
    shape_out = (angles.shape[0],) + (1,) * (values.ndim - 2) + (half_dim,)
    cosine = jnp.cos(angles).reshape(shape_out)
    sine_val = jnp.sin(angles).reshape(shape_out)
    front_half = values[..., :half_dim]
    back_half = values[..., half_dim:]
    return jnp.concatenate(
        [front_half * cosine - back_half * sine_val, back_half * cosine + front_half * sine_val], -1
    )


def rms_norm(tokens, norm_gain):
    wide_tokens = tokens.astype(jnp.float32)
    row_scale = lax.rsqrt(jnp.mean(wide_tokens * wide_tokens, -1, keepdims=True) + 1e-05)
    return (wide_tokens * row_scale * norm_gain).astype(jnp.bfloat16)


def attend_keys(carried, key_block_set, queries, query_pos, query_doc, doc_ends):
    key_block, value_block, key_pos = key_block_set
    key_doc = jnp.sum((key_pos[:, None] >= doc_ends[None, :]).astype(jnp.int32), 1)
    allowed = (key_doc[None, :] == query_doc[:, None]) & (key_pos[None, :] <= query_pos[:, None])
    scale_factor = queries.shape[-1] ** (-0.5)
    running_max, running_sum, weighted = carried
    scores = (
        jnp.einsum("qgjd,kgd->gjqk", queries, key_block, preferred_element_type=jnp.float32)
        * scale_factor
    )
    scores = jnp.where(allowed[None, None], scores, NEG_FILL)
    new_max = jnp.maximum(running_max, jnp.max(scores, -1))
    weights = jnp.where(allowed[None, None], jnp.exp(scores - new_max[..., None]), 0.0)
    rescale = jnp.exp(running_max - new_max)
    new_sum = running_sum * rescale + jnp.sum(weights, -1)
    new_weighted = weighted * rescale[..., None] + jnp.einsum(
        "gjqk,kgd->gjqd",
        weights.astype(jnp.bfloat16),
        value_block,
        preferred_element_type=jnp.float32,
    )
    return (new_max, new_sum, new_weighted)


def make_fold(queries, query_pos, query_doc, doc_ends):

    def fold_keys(carried, pieces, offset):
        key_rows = pieces[0].shape[0]
        step_count = key_rows // BLOCK_KEYS
        stacked = tuple(
            (member.reshape((step_count, BLOCK_KEYS) + member.shape[1:]) for member in pieces)
        )

        def scan_step(softmax_state, key_block_set):
            return (
                attend_keys(softmax_state, key_block_set, queries, query_pos, query_doc, doc_ends),
                None,
            )

        final_state, unused = lax.scan(scan_step, carried, stacked)
        return final_state

    return fold_keys


def local(tokens, norm_gain, w_query, w_key, w_value, w_out, row_map, doc_lengths, doc_labels):
    tok_rows = tokens.shape[0]
    kv_local = w_key.shape[1] // HEAD_DIM
    group_size = HEADS // KV_HEADS
    normed = rms_norm(tokens, norm_gain)
    weight_pieces = (
        lax.all_gather(w_query, "ctx", axis=0, tiled=True),
        lax.all_gather(w_key, "ctx", axis=0, tiled=True),
        lax.all_gather(w_value, "ctx", axis=0, tiled=True),
    )
    queries, key_proj, value_proj = tuple(
        (
            jnp.dot(normed, weight_piece, preferred_element_type=jnp.float32)
            for weight_piece in weight_pieces
        )
    )
    doc_index, in_doc, doc_ends = doc_layout(row_map, doc_lengths)
    queries = rotate(queries.reshape(tok_rows, kv_local, group_size, HEAD_DIM), in_doc).astype(
        jnp.bfloat16
    )
    key_proj = rotate(key_proj.reshape(tok_rows, kv_local, HEAD_DIM), in_doc).astype(jnp.bfloat16)
    value_proj = value_proj.reshape(tok_rows, kv_local, HEAD_DIM).astype(jnp.bfloat16)
    initial = (
        jnp.full((kv_local, group_size, tok_rows), NEG_FILL, jnp.float32),
        jnp.zeros((kv_local, group_size, tok_rows), jnp.float32),
        jnp.zeros((kv_local, group_size, tok_rows, HEAD_DIM), jnp.float32),
    )
    fold_keys = make_fold(queries, row_map, doc_index, doc_ends)
    softmax_state = fold_keys(
        initial,
        (
            lax.all_gather(key_proj, "ctx", axis=0, tiled=True),
            lax.all_gather(value_proj, "ctx", axis=0, tiled=True),
            lax.all_gather(row_map, "ctx", axis=0, tiled=True),
        ),
        jnp.int32(0),
    )
    running_max, running_sum, weighted = softmax_state
    attended = weighted / running_sum[..., None]
    attended = (
        jnp.transpose(attended, (2, 0, 1, 3))
        .reshape(tok_rows, kv_local * group_size * HEAD_DIM)
        .astype(jnp.bfloat16)
    )
    partial_out = jnp.dot(
        attended,
        lax.all_gather(w_out, "ctx", axis=1, tiled=True),
        preferred_element_type=jnp.float32,
    )
    head_share = lax.psum_scatter(
        partial_out.astype(jnp.bfloat16), "head", scatter_dimension=1, tiled=True
    ).astype(jnp.float32)
    col_width = head_share.shape[1]
    own_cols = lax.dynamic_slice_in_dim(tokens, lax.axis_index("head") * col_width, col_width, 1)
    residual_out = (own_cols.astype(jnp.float32) + head_share).astype(jnp.bfloat16)
    is_last = row_map[:, None] == (doc_ends - 1)[None, :]
    label_f = doc_labels.astype(jnp.float32)
    harmful = jnp.sum(label_f)
    harmless = doc_labels.shape[0] - jnp.sum(label_f)
    stream = residual_out.astype(jnp.float32)
    harm_rows = jnp.sum(jnp.where(is_last, label_f[None, :], 0.0), 1)
    safe_rows = jnp.sum(jnp.where(is_last, (1.0 - label_f)[None, :], 0.0), 1)
    harm_sum, safe_sum = lax.psum(
        (jnp.sum(harm_rows[:, None] * stream, 0), jnp.sum(safe_rows[:, None] * stream, 0)), "ctx"
    )
    refusal_direction = harm_sum / harmful - safe_sum / harmless
    return (residual_out, refusal_direction)


def solution(mesh):
    placed = (
        P("ctx", None),
        P(),
        P("ctx", "head"),
        P("ctx", "head"),
        P("ctx", "head"),
        P("head", "ctx"),
        P("ctx"),
        P(),
        P(),
    )
    return jax.shard_map(
        local, mesh=mesh, in_specs=placed, out_specs=(P("ctx", "head"), P("head")), check_vma=False
    )
```

profile of v0, /device:TPU:1, one launch (start us, length us, event | category | flops | bytes accessed | tf_op | source)
XLA Modules:
  0.0 1057.2 jit_solution(1660407853010582978)
XLA Ops:
  11.1 1.5 fusion.19
  13.3 143.4 %all-gather.9.cloned.1.call-done = bf16[4096,128]{1,0:T(8,128)(2,1)} async-done(((bf16[64,128]{1,0:T(8,128)(2,1)}), bf16[4096,128]{1,0:T(8,128)(2,1)}) %all-gather.9.cloned.1.call-update) | async-done | bytes 1048592 | tf_op jit(solution)/shard_map/all_gather | solution.py:99
  156.8 2.2 convolution_bitcast_fusion.1
  160.4 134.9 %all-gather.15.cloned.1.call-done = bf16[4096,128]{1,0:T(8,128)(2,1)} async-done(((bf16[64,128]{1,0:T(8,128)(2,1)}), bf16[4096,128]{1,0:T(8,128)(2,1)}) %all-gather.15.cloned.1.call-update) | async-done | bytes 1048592 | tf_op jit(solution)/shard_map/all_gather | solution.py:100
  295.4 2.3 convolution_convert_fusion.1
  298.7 74.1 %all-gather.1 = s32[64,1,128]{2,1,0:T(1,128)S(1)} all-gather(s32[1,1,128]{2,1,0:T(1,128)S(1)} %bitcast.82), channel_id=1, replica_groups=mesh['ctx'=64,'head'=8] {'ctx'}, dimensions={0}, use_global_device_ids=true | all-gather | bytes 33280 | tf_op jit(solution)/shard_map/all_gather | solution.py:125
  374.1 57.8 %all-gather.11.cloned.1.call-done = bf16[8192,1,128]{0,2,1:T(8,128)(2,1)} async-done(((bf16[128,1,128]{0,2,1:T(8,128)(2,1)}), bf16[8192,1,128]{0,2,1:T(8,128)(2,1)}) %all-gather.11.cloned.1.call-update) | async-done | bytes 2097168 | tf_op jit(solution)/shard_map/all_gather | solution.py:123
  431.9 4.1 copy.39
  436.0 144.2 %all-gather.13.cloned.1.call-done = bf16[4096,512]{1,0:T(8,128)(2,1)} async-done(((bf16[64,512]{1,0:T(8,128)(2,1)}), bf16[4096,512]{1,0:T(8,128)(2,1)}) %all-gather.13.cloned.1.call-update) | async-done | bytes 4194320 | tf_op jit(solution)/shard_map/all_gather | solution.py:98
  580.1 2.9 fusion.35
  583.6 138.0 %all-gather.19.cloned.1.call-done = bf16[8192,128]{1,0:T(8,128)(2,1)} async-done(((bf16[128,128]{1,0:T(8,128)(2,1)}), bf16[8192,128]{1,0:T(8,128)(2,1)}) %all-gather.19.cloned.1.call-update) | async-done | bytes 2097168 | tf_op jit(solution)/shard_map/all_gather | solution.py:124
  721.6 50.8 %while.15 = (s32[]{:T(128)}, f32[1,4,128]{2,1,0:T(4,128)S(1)}, f32[1,4,128]{2,1,0:T(4,128)S(1)}, f32[1,4,128,128]{3,2,1,0:T(8,128)S(1)}, s32[16,512]{1,0:T(8,128...) while((s32[]{:T(128)}, f32[1,4,128]{2,1,0:T(4,128)S(1)}, ...), condition=%wide.region_8.9_spmd.clone, body=%wide.region_4.8_spmd.clone.sunk | while | flops 137021952 | bytes 4372749 | solution.py:86
  726.3 1.4 fusion.57
  729.5 1.4 fusion.57
  732.6 1.4 fusion.57
  735.8 1.4 fusion.57
  739.0 1.4 fusion.57
  742.2 1.4 fusion.57
  745.3 1.4 fusion.57
  748.5 1.4 fusion.57
  751.7 1.4 fusion.57
  754.9 1.4 fusion.57
  758.0 1.4 fusion.57
  761.2 1.4 fusion.57
  764.4 1.4 fusion.57
  767.6 1.4 fusion.57
  770.7 1.3 fusion.57
  772.5 97.7 %all-gather.17.cloned.1.call-done = bf16[512,4096]{0,1:T(8,128)(2,1)} async-done(((bf16[512,64]{0,1:T(8,128)(2,1)}), bf16[512,4096]{0,1:T(8,128)(2,1)}) %all-gather.17.cloned.1.call-update) | async-done | bytes 4194320 | tf_op jit(solution)/shard_map/all_gather | solution.py:138
  870.2 4.7 convolution_convert_fusion
  876.2 37.1 %reduce-scatter.2.cloned.1.call-done = bf16[128,512]{1,0:T(8,128)(2,1)} async-done(((bf16[128,4096]{1,0:T(8,128)(2,1)}), bf16[128,512]{1,0:T(8,128)(2,1)}) %reduce-scatter.2.cloned.1.call-update) | async-done | bytes 131088 | tf_op jit(solution)/shard_map/reduce_scatter | solution.py:141
  913.3 1.6 fusion.22
  914.9 134.3 %all-reduce = (f32[512]{0:T(512)S(1)}, f32[512]{0:T(512)S(1)}) all-reduce(f32[512]{0:T(512)S(1)} %get-tuple-element.143, f32[512]{0:T(512)S(1)} %get-tuple-element.142), channel_id=1, replica_groups=mesh['ctx'=64,'head'=8] {'ctx'}, use_global_device_ids=true, to_apply=%region_16.17 | all-reduce | flops 1024 | bytes 8192 | tf_op jit(solution)/shard_map/psum | solution.py:154
  (179 shorter events, 40.2 us)
Async XLA Ops:
  7.2 288.2 %copy-start = (bf16[128,4096]{1,0:T(8,128)(2,1)S(1)}, bf16[128,4096]{1,0:T(8,128)(2,1)}, u32[]{:S(2)}) copy-start(bf16[128,4096]{1,0:T(8,128)(2,1)} %param.11) | copy-start | bytes 3145732
  7.2 288.2 %copy-start.2 = (f32[4096]{0:T(1024)S(1)}, f32[4096]{0:T(1024)}, u32[]{:S(2)}) copy-start(f32[4096]{0:T(1024)} %param.12) | copy-start | bytes 49156
  7.2 149.6 %all-gather.9.cloned.1.call-start = ((), (), s32[]{:S(2)}) async-start(), calls=%async_computation.1 | async-start | bytes 1064960 | tf_op jit(solution)/shard_map/all_gather | solution.py:99
  7.9 287.5 %all-gather.15.cloned.1.call-start = ((), (), s32[]{:S(2)}) async-start(), calls=%async_computation.4 | async-start | bytes 1064960 | tf_op jit(solution)/shard_map/all_gather | solution.py:100
  8.7 423.2 %all-gather.11.cloned.1.call-start = ((), (), s32[]{:S(2)}) async-start(), calls=%async_computation.2 | async-start | bytes 2129920 | tf_op jit(solution)/shard_map/all_gather | solution.py:123
  158.9 139.8 %copy-start.1 = (s32[128]{0:T(128)S(1)}, s32[128]{0:T(128)}, u32[]{:S(2)}) copy-start(s32[128]{0:T(128)} %param.17) | copy-start | bytes 1540
  159.8 420.3 %all-gather.13.cloned.1.call-start = ((), (), s32[]{:S(2)}) async-start(), calls=%async_computation.3 | async-start | bytes 4259840 | tf_op jit(solution)/shard_map/all_gather | solution.py:98
  160.4 561.2 %all-gather.19.cloned.1.call-start = ((), (), s32[]{:S(2)}) async-start(), calls=%async_computation.7 | async-start | bytes 2129920 | tf_op jit(solution)/shard_map/all_gather | solution.py:124
  297.7 572.5 %all-gather.17.cloned.1.call-start = ((), (), s32[]{:S(2)}) async-start(), calls=%async_computation.5 | async-start | bytes 4259840 | tf_op jit(solution)/shard_map/all_gather | solution.py:138
  298.3 615.0 %reduce-scatter.2.cloned.1.call-start = ((), (), s32[]{:S(2)}) async-start(), calls=%async_computation.6 | async-start | bytes 1179648 | tf_op jit(solution)/shard_map/reduce_scatter | solution.py:141
  870.2 4.7 copy-start.3
Sparse Core Ops, SparseCore 0:
  11.3 145.4 all-gather.8
  160.1 135.2 all-gather.14
  299.0 132.8 all-gather.10
  435.0 145.0 all-gather.12
  583.3 138.2 all-gather.18
  724.7 145.4 all-gather.16
  875.0 38.2 reduce-scatter.1
where the time goes:
time: 1060 us
  waiting for transfers between devices  756 us (71%)
  blocking collectives  208 us (20%)
  matrix products  53.2 us (5%)
  other arithmetic  17.8 us (2%)
  between operations  14.9 us (1%)
    all_gather x1, waiting for transfers between devices, local(): lax.all_gather(w_query, 'ctx', axis=0, tiled=True)  144 us
    all_gather x1, waiting for transfers between devices, local(): lax.all_gather(w_key, 'ctx', axis=0, tiled=True)  143 us
    all_gather x1, waiting for transfers between devices, local(): lax.all_gather(value_proj, 'ctx', axis=0, tiled=True)  138 us
    all_gather x1, waiting for transfers between devices, local(): lax.all_gather(w_value, 'ctx', axis=0, tiled=True)  135 us
    psum x1, blocking collectives, local(): lax.psum((jnp.sum(harm_rows[:, None] * stream, 0), jnp.sum(safe_rows[:, N...  134 us
    all_gather x1, waiting for transfers between devices, local(): lax.all_gather(w_out, 'ctx', axis=1, tiled=True)  97.7 us
    all_gather x1, blocking collectives, local(): lax.all_gather(row_map, 'ctx', axis=0, tiled=True)  74.1 us
    all_gather x1, waiting for transfers between devices, local(): lax.all_gather(key_proj, 'ctx', axis=0, tiled=True)  57.8 us
  transfers between devices with their start and end apart: 7, of which 7 were waited for; matrix products, arithmetic and copies ran while one was open for 7% of the time, Pallas kernels for 0%

commit v1 on v0

--- a/solution.py
+++ b/solution.py
@@ -90,6 +90,15 @@
 
 
 def local(tokens, norm_gain, w_query, w_key, w_value, w_out, row_map, doc_lengths, doc_labels):
+
+    def _bind_forms(bus_axis, state):
+        val = lax.axis_size(bus_axis)
+        inter = jnp.stack(val * [state])
+        f_next = jnp.concatenate(
+            lax.all_to_all(inter, bus_axis, split_axis=0, concat_axis=0), axis=0
+        )
+        return f_next
+
     tok_rows = tokens.shape[0]
     kv_local = w_key.shape[1] // HEAD_DIM
     group_size = HEADS // KV_HEADS
@@ -121,7 +130,7 @@
         initial,
         (
             lax.all_gather(key_proj, "ctx", axis=0, tiled=True),
-            lax.all_gather(value_proj, "ctx", axis=0, tiled=True),
+            _bind_forms("ctx", value_proj),
             lax.all_gather(row_map, "ctx", axis=0, tiled=True),
         ),
         jnp.int32(0),

time: 1060 us -> 952 us (0.90)
  waiting for transfers between devices: 756 us -> 553 us
  blocking collectives: 208 us -> 293 us
    all_gather x1 -> x0, waiting for transfers between devices: 138 us -> none  [local(): lax.all_gather(value_proj, 'ctx', axis=0, tiled=True)]
    all_gather x1, blocking collectives: 74.1 us -> 159 us  [local(): lax.all_gather(row_map, 'ctx', axis=0, tiled=True)]
    all_gather x1, waiting for transfers between devices: 57.8 us -> 0.02 us  [local(): lax.all_gather(key_proj, 'ctx', axis=0, tiled=True)]
  transfers between devices with their start and end apart: 7 -> 7, of which waited for: 7 -> 5; matrix products, arithmetic and copies ran while one was open for 7% -> 7% of each run, Pallas kernels for 0% -> 0%
where the time goes in v1:
time: 952 us; the launch traced here: 951 us
  waiting for transfers between devices  553 us (58%)
  blocking collectives  293 us (31%)
  matrix products  52.8 us (6%)
  other arithmetic  17.8 us (2%)
  between operations  14.9 us (2%)
  starting transfers between devices  10.2 us (1%)
    all_gather x1, blocking collectives, local(): lax.all_gather(row_map, 'ctx', axis=0, tiled=True)  159 us
    all_gather x1, waiting for transfers between devices, local(): lax.all_gather(w_key, 'ctx', axis=0, tiled=True)  143 us
    all_gather x1, waiting for transfers between devices, local(): lax.all_gather(w_query, 'ctx', axis=0, tiled=True)  141 us
    all_gather x1, waiting for transfers between devices, local(): lax.all_gather(w_value, 'ctx', axis=0, tiled=True)  135 us
    psum x1, blocking collectives, local(): lax.psum((jnp.sum(harm_rows[:, None] * stream, 0), jnp.sum(safe_rows[:, N...  134 us
    all_gather x1, waiting for transfers between devices, local(): lax.all_gather(w_out, 'ctx', axis=1, tiled=True)  94.2 us
    reduce_scatter x1, waiting for transfers between devices, local(): lax.psum_scatter(partial_out.astype(jnp.bfloat16), 'head', scatter_dimens...  37.1 us
    dot_general x16, matrix products, attend_keys(): jnp.einsum('gjqk,kgd->gjqd', weights.astype(jnp.bfloat16), value_block, p...  21.7 us
  transfers between devices with their start and end apart: 7, of which 5 were waited for; matrix products, arithmetic and copies ran while one was open for 7% of the time, Pallas kernels for 0%

profile of v1, /device:TPU:1, one launch (start us, length us, event | category | flops | bytes accessed | tf_op | source)
XLA Modules:
  0.0 950.9 jit_solution(5463650271351038007)
XLA Ops:
  11.1 1.5 fusion.19
  13.3 143.4 %all-gather.7.cloned.1.call-done = bf16[4096,128]{1,0:T(8,128)(2,1)} async-done(((bf16[64,128]{1,0:T(8,128)(2,1)}), bf16[4096,128]{1,0:T(8,128)(2,1)}) %all-gather.7.cloned.1.call-update) | async-done | bytes 1048592 | tf_op jit(solution)/shard_map/all_gather | solution.py:108
  156.8 2.2 convolution_bitcast_fusion.1
  160.4 135.0 %all-gather.13.cloned.1.call-done = bf16[4096,128]{1,0:T(8,128)(2,1)} async-done(((bf16[64,128]{1,0:T(8,128)(2,1)}), bf16[4096,128]{1,0:T(8,128)(2,1)}) %all-gather.13.cloned.1.call-update) | async-done | bytes 1048592 | tf_op jit(solution)/shard_map/all_gather | solution.py:109
  295.4 1.7 convolution_convert_fusion.1
  297.1 1.9 stack.2
  299.0 9.9 %all-to-all-start = ((bf16[64,128,1,128]{3,1,2,0:T(8,128)(2,1)}), bf16[64,128,1,128]{3,1,2,0:T(8,128)(2,1)}, u32[]{:S(2)}, u32[]{:S(2)}) async-start(bf16[64,128,1,128]{3,1,2,0:T(8,128)(2,1)} %stack.2), calls=%async_computation | async-start | bytes 4194304 | tf_op jit(solution)/shard_map/all_to_all | solution.py:98
  309.6 158.9 %all-gather = s32[64,1,128]{2,1,0:T(1,128)S(1)} all-gather(s32[1,1,128]{2,1,0:T(1,128)S(1)} %bitcast.81), channel_id=1, replica_groups=mesh['ctx'=64,'head'=8] {'ctx'}, dimensions={0}, use_global_device_ids=true | all-gather | bytes 33280 | tf_op jit(solution)/shard_map/all_gather | solution.py:134
  470.2 4.1 copy.37
  474.3 140.8 %all-gather.11.cloned.1.call-done = bf16[4096,512]{1,0:T(8,128)(2,1)} async-done(((bf16[64,512]{1,0:T(8,128)(2,1)}), bf16[4096,512]{1,0:T(8,128)(2,1)}) %all-gather.11.cloned.1.call-update) | async-done | bytes 4194320 | tf_op jit(solution)/shard_map/all_gather | solution.py:107
  615.1 2.9 fusion.35
  618.6 50.9 %while.15 = (s32[]{:T(128)}, f32[1,4,128]{2,1,0:T(4,128)S(1)}, f32[1,4,128]{2,1,0:T(4,128)S(1)}, f32[1,4,128,128]{3,2,1,0:T(8,128)S(1)}, s32[16,512]{1,0:T(8,128...) while((s32[]{:T(128)}, f32[1,4,128]{2,1,0:T(4,128)S(1)}, ...), condition=%wide.region_8.9_spmd.clone, body=%wide.region_4.8_spmd.clone.sunk | while | flops 137021952 | bytes 4372749 | solution.py:86
  623.3 1.4 fusion.57
  626.5 1.4 fusion.57
  629.7 1.4 fusion.57
  632.9 1.4 fusion.57
  636.1 1.4 fusion.57
  639.2 1.4 fusion.57
  642.4 1.4 fusion.57
  645.6 1.4 fusion.57
  648.8 1.4 fusion.57
  652.0 1.4 fusion.57
  655.1 1.4 fusion.57
  658.3 1.4 fusion.57
  661.5 1.4 fusion.57
  664.7 1.4 fusion.57
  667.9 1.4 fusion.57
  669.6 94.2 %all-gather.15.cloned.1.call-done = bf16[512,4096]{0,1:T(8,128)(2,1)} async-done(((bf16[512,64]{0,1:T(8,128)(2,1)}), bf16[512,4096]{0,1:T(8,128)(2,1)}) %all-gather.15.cloned.1.call-update) | async-done | bytes 4194320 | tf_op jit(solution)/shard_map/all_gather | solution.py:147
  763.9 4.7 convolution_convert_fusion
  769.9 37.1 %reduce-scatter.2.cloned.1.call-done = bf16[128,512]{1,0:T(8,128)(2,1)} async-done(((bf16[128,4096]{1,0:T(8,128)(2,1)}), bf16[128,512]{1,0:T(8,128)(2,1)}) %reduce-scatter.2.cloned.1.call-update) | async-done | bytes 131088 | tf_op jit(solution)/shard_map/reduce_scatter | solution.py:150
  807.0 1.6 fusion.22
  808.6 134.3 %all-reduce = (f32[512]{0:T(512)S(1)}, f32[512]{0:T(512)S(1)}) all-reduce(f32[512]{0:T(512)S(1)} %get-tuple-element.143, f32[512]{0:T(512)S(1)} %get-tuple-element.142), channel_id=1, replica_groups=mesh['ctx'=64,'head'=8] {'ctx'}, use_global_device_ids=true, to_apply=%region_16.17 | all-reduce | flops 1024 | bytes 8192 | tf_op jit(solution)/shard_map/psum | solution.py:163
  (179 shorter events, 40.3 us)
Async XLA Ops:
  7.2 288.2 %copy-start = (bf16[128,4096]{1,0:T(8,128)(2,1)S(1)}, bf16[128,4096]{1,0:T(8,128)(2,1)}, u32[]{:S(2)}) copy-start(bf16[128,4096]{1,0:T(8,128)(2,1)} %param.11) | copy-start | bytes 3145732
  7.2 288.2 %copy-start.2 = (f32[4096]{0:T(1024)S(1)}, f32[4096]{0:T(1024)}, u32[]{:S(2)}) copy-start(f32[4096]{0:T(1024)} %param.12) | copy-start | bytes 49156
  7.2 149.6 %all-gather.7.cloned.1.call-start = ((), (), s32[]{:S(2)}) async-start(), calls=%async_computation.2 | async-start | bytes 1064960 | tf_op jit(solution)/shard_map/all_gather | solution.py:108
  7.9 287.5 %all-gather.13.cloned.1.call-start = ((), (), s32[]{:S(2)}) async-start(), calls=%async_computation.5 | async-start | bytes 1064960 | tf_op jit(solution)/shard_map/all_gather | solution.py:109
  8.7 461.5 %all-gather.9.cloned.1.call-start = ((), (), s32[]{:S(2)}) async-start(), calls=%async_computation.3 | async-start | bytes 2129920 | tf_op jit(solution)/shard_map/all_gather | solution.py:132
  159.8 455.3 %all-gather.11.cloned.1.call-start = ((), (), s32[]{:S(2)}) async-start(), calls=%async_computation.4 | async-start | bytes 4259840 | tf_op jit(solution)/shard_map/all_gather | solution.py:107
  299.0 10.6 %copy-start.1 = (s32[128]{0:T(128)S(1)}, s32[128]{0:T(128)}, u32[]{:S(2)}) copy-start(s32[128]{0:T(128)} %param.17) | copy-start | bytes 1540
  299.0 319.6 %all-to-all-start = ((bf16[64,128,1,128]{3,1,2,0:T(8,128)(2,1)}), bf16[64,128,1,128]{3,1,2,0:T(8,128)(2,1)}, u32[]{:S(2)}, u32[]{:S(2)}) async-start(bf16[64,128,1,128]{3,1,2,0:T(8,128)(2,1)} %stack.2), calls=%async_computation | async-start | bytes 4194304 | tf_op jit(solution)/shard_map/all_to_all | solution.py:98
  308.9 454.9 %all-gather.15.cloned.1.call-start = ((), (), s32[]{:S(2)}) async-start(), calls=%async_computation.6 | async-start | bytes 4259840 | tf_op jit(solution)/shard_map/all_gather | solution.py:147
  309.5 497.5 %reduce-scatter.2.cloned.1.call-start = ((), (), s32[]{:S(2)}) async-start(), calls=%async_computation.7 | async-start | bytes 1179648 | tf_op jit(solution)/shard_map/reduce_scatter | solution.py:150
  763.9 4.7 copy-start.3
Sparse Core Ops, SparseCore 0:
  11.3 145.4 all-gather.6
  160.1 135.2 all-gather.12
  299.0 168.1 all-gather.8
  470.3 144.8 all-gather.10
  618.3 145.5 all-gather.14
  768.7 38.2 reduce-scatter.1
